TPU v7x, 512 devices: a whole 4x8x8 slice. The times are simulated.
512 devices in a mesh: dp: 8 (over y_lo, core), gx: 64 (over y_hi, z, x).
Axes of the slice: x: 4, y: 8 (y_hi: 2, y_lo: 4; y = y_hi * 4 + y_lo), z: 8, core: 2. Of those that a mesh axis runs over, the one named last changes fastest.
Arguments:
- features: bfloat16 [8, 16, 128, 8, 256], P('dp', None, 'gx'), may hold values from -6 to 6
- offsets: int32 [8, 3], P('dp'), may hold values from 0 to 255, as said below
- flip_bits: int32 [8, 3], P('dp'), may hold values from 0 to 1
- weight: bfloat16 [27, 16, 16], replicated, may hold values from -0.3125 to 0.3125
- conv_bias: float32 [16], replicated, may hold values from -3 to 3
- cotangent: bfloat16 [8, 16, 128, 8, 256], P('dp', None, 'gx'), may hold values from -6 to 6
Outputs:
- hidden: bfloat16 [8, 16, 128, 8, 256], P('dp', None, 'gx')
- grad_input: bfloat16 [8, 16, 128, 8, 256], P('dp', None, 'gx')
- grad_weight: float32 [27, 16, 16], replicated
- grad_bias: float32 [16], replicated
Inputs may be any that keep to these rules, and one draw needn't show every extreme that they name: `offsets`: column 0 lies in 0 to 127, column 1 in 0 to 7, column 2 in 0 to 255.
All inputs are finite; a program needn't handle non-finite values.
Results may differ from a plain program's by a relative error of at most 0.0075.
Values may be sent and summed in bfloat16 or wider, within the bound.
No kernel may reach another device: no remote copies, remote signals or barrier semaphores. Data moves between devices by JAX's collectives and lax.ppermute only.
A program may use at most 64 MiB of HBM per device.

v0:
```python
import math

import jax
import jax.numpy as jnp
from jax import lax
from jax.sharding import PartitionSpec as P

tap_offsets = [
    (shift_x, shift_y, shift_z)
    for shift_x in range(3)
    for shift_y in range(3)
    for shift_z in range(3)
]


def partner_2(block, axis, bit):
    count = lax.axis_size(axis)
    route = []
    for low in range(count):
        high = low | 1 << bit
        if high != low and high < count:
            route += [(low, high), (high, low)]
    return lax.ppermute(block, axis, route)


def shifted(value, axis, steps):
    count = lax.axis_size(axis)
    pairs = [(source, (source + steps) % count) for source in range(count)]
    return lax.ppermute(value, axis, pairs)


def padded_2(shard, sides, width):
    for axis, dim in sides:
        peers, length = (lax.axis_size(axis), shard.shape[dim])
        up = [(i, (i + 1) % peers) for i in range(peers)]
        down = [(j, i) for i, j in up]
        last = lax.slice_in_dim(shard, length - width, length, axis=dim)
        leading = lax.slice_in_dim(shard, 0, width, axis=dim)
        before = lax.ppermute(last, axis, up)
        after = lax.ppermute(leading, axis, down)
        shard = jnp.concatenate([before, shard, after], axis=dim)
    return shard


def permute_axis(volume, offset, mirror_bit, length, dim_index):
    position = jnp.arange(length, dtype=jnp.int32)
    source = jnp.where(mirror_bit == 1, length - 1 - position, position)
    source = jnp.mod(source - offset, length)
    return jnp.take(volume, source, axis=dim_index)


def augment_local(volume, offset, mirror_bits):
    volume = permute_axis(volume, offset[1], mirror_bits[1], volume.shape[2], 2)
    return permute_axis(volume, offset[2], mirror_bits[2], volume.shape[3], 3)


def gelu_parts(pre_act):
    normal_cdf = 0.5 * (1.0 + lax.erf(pre_act * 0.7071067811865476))
    density = jnp.exp(-0.5 * pre_act * pre_act) * 0.3989422804014327
    return (pre_act * normal_cdf, normal_cdf + pre_act * density)


def cut_planes(stacked, begin_at, length):

    def single(volume, first):
        return lax.dynamic_slice_in_dim(volume, first, length, 1)

    return jax.vmap(single)(stacked, begin_at)


def on_device(features, offsets, flip_bits, weight, conv_bias, cotangent):
    planes = features.shape[2]
    devices_x = lax.axis_size("gx")
    levels = devices_x.bit_length() - 1
    length_x = planes * devices_x
    local = jax.vmap(augment_local)(features, offsets, flip_bits)
    mirror_x = (flip_bits[:, 0] == 1)[:, None, None, None, None]
    mirrored = jnp.where(mirror_x, jnp.flip(local, 2), local)
    for bit_level in range(levels):
        partner = partner_2(mirrored, "gx", bit_level)
        mirrored = jnp.where(mirror_x, partner, mirrored)
    effective = jnp.where(flip_bits[:, 0] == 1, jnp.mod(-offsets[:, 0], length_x), offsets[:, 0])
    coarse_steps = effective // planes
    remain = effective % planes
    coarse = mirrored
    for bit_level in range(levels):
        arrived = shifted(coarse, "gx", 2**bit_level)
        taken = (coarse_steps // 2**bit_level % 2 == 1)[:, None, None, None, None]
        coarse = jnp.where(taken, arrived, coarse)
    previous = shifted(coarse, "gx", 1)
    joined = jnp.concatenate([previous, coarse], axis=2)
    augmented = cut_planes(joined, planes - remain, planes)
    padded = padded_2(augmented, (("gx", 2),), 1)
    total = jnp.zeros(features.shape, jnp.float32) + conv_bias[None, :, None, None, None]
    for tap_index, (shift_x, shift_y, shift_z) in enumerate(tap_offsets):
        window = jnp.roll(
            padded[:, :, shift_x : shift_x + planes], (1 - shift_y, 1 - shift_z), axis=(3, 4)
        )
        total = total + jnp.einsum(
            "oi,bixyz->boxyz", weight[tap_index], window, preferred_element_type=jnp.float32
        )
    hidden, slope = gelu_parts(total)
    grad_pre = (cotangent.astype(jnp.float32) * slope).astype(jnp.bfloat16)
    grad_pad = padded_2(grad_pre, (("gx", 2),), 1)
    grad_in = jnp.zeros(features.shape, jnp.float32)
    grad_list = []
    for tap_index, (shift_x, shift_y, shift_z) in enumerate(tap_offsets):
        window = jnp.roll(
            padded[:, :, shift_x : shift_x + planes], (1 - shift_y, 1 - shift_z), axis=(3, 4)
        )
        grad_list.append(
            jnp.einsum("boxyz,bixyz->oi", grad_pre, window, preferred_element_type=jnp.float32)
        )
        moved_grad = jnp.roll(
            grad_pad[:, :, 2 - shift_x : 2 - shift_x + planes],
            (shift_y - 1, shift_z - 1),
            axis=(3, 4),
        )
        grad_in = grad_in + jnp.einsum(
            "oi,boxyz->bixyz", weight[tap_index], moved_grad, preferred_element_type=jnp.float32
        )
    grad_b = jnp.sum(grad_pre.astype(jnp.float32), axis=(0, 2, 3, 4))
    summed_w, summed_b = lax.psum((jnp.stack(grad_list), grad_b), ("dp", "gx"))
    cell_count = (
        features.shape[0] * lax.axis_size("dp") * length_x * features.shape[3] * features.shape[4]
    )
    grad_scale = 1.0 / math.sqrt(cell_count)
    return (
        hidden.astype(jnp.bfloat16),
        grad_in.astype(jnp.bfloat16),
        summed_w * grad_scale,
        summed_b * grad_scale,
    )


def solution(mesh):
    in_specs = (
        P("dp", None, "gx", None, None),
        P("dp", None),
        P("dp", None),
        P(),
        P(),
        P("dp", None, "gx", None, None),
    )
    out_specs = (P("dp", None, "gx", None, None), P("dp", None, "gx", None, None), P(), P())
    return jax.shard_map(
        on_device, mesh=mesh, in_specs=in_specs, out_specs=out_specs, check_vma=False
    )
```

profile of v0, /device:TPU:1, one launch (start us, length us, event | category | flops | bytes accessed | tf_op | source)
XLA Modules:
  0.0 339.2 jit_solution(17937598453677583954)
XLA Ops:
  0.6 1.4 fusion.388
  11.5 3.9 %collective-permute-start = (bf16[1,16,2,8,256]{4,1,3,2,0:T(8,128)(2,1)S(1)}, bf16[1,16,2,8,256]{4,1,3,2,0:T(8,128)(2,1)S(1)}, u32[]{:S(2)}, u32[]{:S(2)}) collective-permute-start(bf16[1,16,2,8,256]{4,1,3,2,0:T(8,128)(2,1)S(1)} %reverse_select_fusion), channel_id=1, source_target_pairs={{0,1},{1,0},{2,3},{3,2},{4,5},{5,4},{6,7},{7,6},{8,9},{9,8},{10,11... | collective-permute-start | bytes 393224 | tf_op jit(solution)/shard_map/ppermute | solution.py:23
  15.4 2.3 collective-permute-done
  17.8 5.4 %collective-permute-start.1 = (bf16[1,16,2,8,256]{4,1,3,2,0:T(8,128)(2,1)S(1)}, bf16[1,16,2,8,256]{4,1,3,2,0:T(8,128)(2,1)S(1)}, u32[]{:S(2)}, u32[]{:S(2)}) collective-permute-start(bf16[1,16,2,8,256]{4,1,3,2,0:T(8,128)(2,1)S(1)} %broadcast_select_fusion.5), channel_id=1, source_target_pairs={{0,2},{2,0},{1,3},{3,1},{4,6},{6,4},{5,7},{7,5},{8,10},{10,8},{9,1... | collective-permute-start | bytes 393224 | tf_op jit(solution)/shard_map/ppermute | solution.py:23
  23.3 2.3 collective-permute-done.1
  25.6 4.2 %collective-permute-start.2 = (bf16[1,16,2,8,256]{4,1,3,2,0:T(8,128)(2,1)S(1)}, bf16[1,16,2,8,256]{4,1,3,2,0:T(8,128)(2,1)S(1)}, u32[]{:S(2)}, u32[]{:S(2)}) collective-permute-start(bf16[1,16,2,8,256]{4,1,3,2,0:T(8,128)(2,1)S(1)} %broadcast_select_fusion.4), channel_id=1, source_target_pairs={{0,4},{4,0},{1,5},{5,1},{2,6},{6,2},{3,7},{7,3},{8,12},{12,8},{9,1... | collective-permute-start | bytes 393224 | tf_op jit(solution)/shard_map/ppermute | solution.py:23
  29.9 2.6 collective-permute-done.2
  32.5 5.5 %collective-permute-start.3 = (bf16[1,16,2,8,256]{4,1,3,2,0:T(8,128)(2,1)S(1)}, bf16[1,16,2,8,256]{4,1,3,2,0:T(8,128)(2,1)S(1)}, u32[]{:S(2)}, u32[]{:S(2)}) collective-permute-start(bf16[1,16,2,8,256]{4,1,3,2,0:T(8,128)(2,1)S(1)} %broadcast_select_fusion.3), channel_id=1, source_target_pairs={{0,8},{8,0},{1,9},{9,1},{2,10},{10,2},{3,11},{11,3},{4,12},{12,4},... | collective-permute-start | bytes 393224 | tf_op jit(solution)/shard_map/ppermute | solution.py:23
  38.0 3.8 %collective-permute-done.3 = bf16[1,16,2,8,256]{4,1,3,2,0:T(8,128)(2,1)S(1)} collective-permute-done((bf16[1,16,2,8,256]{4,1,3,2,0:T(8,128)(2,1)S(1)}, bf16[1,16,2,8,256]{4,1,3,2,0:T(8,128)(2,1)S(1)}, u32[]{:S(2)}, u32[]{:S(2)}) %collective-permute-start.3) | collective-permute-done | bytes 131104 | tf_op jit(solution)/shard_map/ppermute | solution.py:23
  41.9 8.4 %collective-permute-start.4 = (bf16[1,16,2,8,256]{4,1,3,2,0:T(8,128)(2,1)S(1)}, bf16[1,16,2,8,256]{4,1,3,2,0:T(8,128)(2,1)S(1)}, u32[]{:S(2)}, u32[]{:S(2)}) collective-permute-start(bf16[1,16,2,8,256]{4,1,3,2,0:T(8,128)(2,1)S(1)} %broadcast_select_fusion.2), channel_id=1, source_target_pairs={{0,16},{16,0},{1,17},{17,1},{2,18},{18,2},{3,19},{19,3},{4,20},{20... | collective-permute-start | bytes 393224 | tf_op jit(solution)/shard_map/ppermute | solution.py:23
  50.3 2.4 collective-permute-done.4
  52.7 7.5 %collective-permute-start.5 = (bf16[1,16,2,8,256]{4,1,3,2,0:T(8,128)(2,1)S(1)}, bf16[1,16,2,8,256]{4,1,3,2,0:T(8,128)(2,1)S(1)}, u32[]{:S(2)}, u32[]{:S(2)}) collective-permute-start(bf16[1,16,2,8,256]{4,1,3,2,0:T(8,128)(2,1)S(1)} %broadcast_select_fusion.1), channel_id=1, source_target_pairs={{0,32},{32,0},{1,33},{33,1},{2,34},{34,2},{3,35},{35,3},{4,36},{36... | collective-permute-start | bytes 393224 | tf_op jit(solution)/shard_map/ppermute | solution.py:23
  60.2 2.4 collective-permute-done.5
  62.6 3.1 collective-permute-start.6
  67.7 15.7 %collective-permute-done.6 = bf16[1,16,2,8,256]{4,1,3,2,0:T(8,128)(2,1)S(1)} collective-permute-done((bf16[1,16,2,8,256]{4,1,3,2,0:T(8,128)(2,1)S(1)}, bf16[1,16,2,8,256]{4,1,3,2,0:T(8,128)(2,1)S(1)}, u32[]{:S(2)}, u32[]{:S(2)}) %collective-permute-start.6) | collective-permute-done | bytes 131104 | tf_op jit(solution)/shard_map/ppermute | solution.py:29
  83.4 1.9 collective-permute-start.7
  85.4 12.2 %collective-permute-done.7 = bf16[1,16,2,8,256]{4,1,3,2,0:T(8,128)(2,1)S(1)} collective-permute-done((bf16[1,16,2,8,256]{4,1,3,2,0:T(8,128)(2,1)S(1)}, bf16[1,16,2,8,256]{4,1,3,2,0:T(8,128)(2,1)S(1)}, u32[]{:S(2)}, u32[]{:S(2)}) %collective-permute-start.7) | collective-permute-done | bytes 131104 | tf_op jit(solution)/shard_map/ppermute | solution.py:29
  97.6 1.9 collective-permute-start.8
  99.5 9.8 %collective-permute-done.8 = bf16[1,16,2,8,256]{4,1,3,2,0:T(8,128)(2,1)S(1)} collective-permute-done((bf16[1,16,2,8,256]{4,1,3,2,0:T(8,128)(2,1)S(1)}, bf16[1,16,2,8,256]{4,1,3,2,0:T(8,128)(2,1)S(1)}, u32[]{:S(2)}, u32[]{:S(2)}) %collective-permute-start.8) | collective-permute-done | bytes 131104 | tf_op jit(solution)/shard_map/ppermute | solution.py:29
  109.3 1.9 collective-permute-start.9
  111.3 10.7 %collective-permute-done.9 = bf16[1,16,2,8,256]{4,1,3,2,0:T(8,128)(2,1)S(1)} collective-permute-done((bf16[1,16,2,8,256]{4,1,3,2,0:T(8,128)(2,1)S(1)}, bf16[1,16,2,8,256]{4,1,3,2,0:T(8,128)(2,1)S(1)}, u32[]{:S(2)}, u32[]{:S(2)}) %collective-permute-start.9) | collective-permute-done | bytes 131104 | tf_op jit(solution)/shard_map/ppermute | solution.py:29
  122.0 1.9 collective-permute-start.10
  124.0 12.4 %collective-permute-done.10 = bf16[1,16,2,8,256]{4,1,3,2,0:T(8,128)(2,1)S(1)} collective-permute-done((bf16[1,16,2,8,256]{4,1,3,2,0:T(8,128)(2,1)S(1)}, bf16[1,16,2,8,256]{4,1,3,2,0:T(8,128)(2,1)S(1)}, u32[]{:S(2)}, u32[]{:S(2)}) %collective-permute-start.10) | collective-permute-done | bytes 131104 | tf_op jit(solution)/shard_map/ppermute | solution.py:29
  136.4 8.2 %collective-permute-start.11 = (bf16[1,16,2,8,256]{4,1,3,2,0:T(8,128)(2,1)S(1)}, bf16[1,16,2,8,256]{4,1,3,2,0:T(8,128)(2,1)S(1)}, u32[]{:S(2)}, u32[]{:S(2)}) collective-permute-start(bf16[1,16,2,8,256]{4,1,3,2,0:T(8,128)(2,1)S(1)} %broadcast_select_fusion.10), channel_id=1, source_target_pairs={{0,32},{1,33},{2,34},{3,35},{4,36},{5,37},{6,38},{7,39},{8,40},{9,... | collective-permute-start | bytes 393224 | tf_op jit(solution)/shard_map/ppermute | solution.py:29
  147.0 1.9 collective-permute-start.12
  152.8 8.1 %collective-permute-done.12 = bf16[1,16,2,8,256]{4,1,3,2,0:T(8,128)(2,1)S(1)} collective-permute-done((bf16[1,16,2,8,256]{4,1,3,2,0:T(8,128)(2,1)S(1)}, bf16[1,16,2,8,256]{4,1,3,2,0:T(8,128)(2,1)S(1)}, u32[]{:S(2)}, u32[]{:S(2)}) %collective-permute-start.12) | collective-permute-done | bytes 131104 | tf_op jit(solution)/shard_map/ppermute | solution.py:29
  160.9 1.9 collective-permute-start.13
  162.8 11.5 %collective-permute-start.14 = (bf16[1,16,1,8,256]{4,1,3,2,0:T(8,128)(2,1)S(1)}, bf16[1,16,1,8,256]{4,1,3,2,0:T(8,128)(2,1)S(1)}, u32[]{:S(2)}, u32[]{:S(2)}) collective-permute-start(bf16[1,16,1,8,256]{4,1,3,2,0:T(8,128)(2,1)S(1)} %get-tuple-element.128), channel_id=1, source_target_pairs={{1,0},{2,1},{3,2},{4,3},{5,4},{6,5},{7,6},{8,7},{9,8},{10,9},{11,1... | collective-permute-start | bytes 196616 | tf_op jit(solution)/shard_map/ppermute | solution.py:40
  189.3 122.1 %all-reduce = (f32[27,16,16]{2,1,0:T(8,128)S(1)}, f32[16]{0:T(128)S(1)}) all-reduce(f32[27,16,16]{2,1,0:T(8,128)S(1)} %fusion.42, f32[16]{0:T(128)S(1)} %get-tuple-element.25), channel_id=1, replica_groups=mesh['dp'=8,'gx'=64] {'dp','gx'}, use_global_device_ids=true, to_apply=%region_0.1 | all-reduce | flops 6928 | bytes 55424 | tf_op jit(solution)/shard_map/psum | solution.py:123
  311.4 5.0 %collective-permute-start.15 = (bf16[1,16,1,8,256]{4,1,3,2,0:T(8,128)(2,1)S(1)}, bf16[1,16,1,8,256]{4,1,3,2,0:T(8,128)(2,1)S(1)}, u32[]{:S(2)}, u32[]{:S(2)}) collective-permute-start(bf16[1,16,1,8,256]{4,1,3,2,0:T(8,128)(2,1)S(1)} %get-tuple-element.95), channel_id=1, source_target_pairs={{1,0},{2,1},{3,2},{4,3},{5,4},{6,5},{7,6},{8,7},{9,8},{10,9},{11,1... | collective-permute-start | bytes 196616 | tf_op jit(solution)/shard_map/ppermute | solution.py:40
  316.4 1.9 collective-permute-start.16
  320.4 9.7 %collective-permute-done.16 = bf16[1,16,1,8,256]{4,1,3,2,0:T(8,128)(2,1)S(1)} collective-permute-done((bf16[1,16,1,8,256]{4,1,3,2,0:T(8,128)(2,1)S(1)}, bf16[1,16,1,8,256]{4,1,3,2,0:T(8,128)(2,1)S(1)}, u32[]{:S(2)}, u32[]{:S(2)}) %collective-permute-start.16) | collective-permute-done | bytes 65568 | tf_op jit(solution)/shard_map/ppermute | solution.py:39
  (186 shorter events, 39.4 us)
Async XLA Ops:
  0.6 7.4 %copy-start = (bf16[1,16,2,8,256]{4,3,2,1,0:T(8,128)(2,1)S(1)}, bf16[1,16,2,8,256]{4,3,2,1,0:T(8,128)(2,1)}, u32[]{:S(2)}) copy-start(bf16[1,16,2,8,256]{4,3,2,1,0:T(8,128)(2,1)} %param.6) | copy-start | bytes 393220
  11.5 6.3 %collective-permute-start = (bf16[1,16,2,8,256]{4,1,3,2,0:T(8,128)(2,1)S(1)}, bf16[1,16,2,8,256]{4,1,3,2,0:T(8,128)(2,1)S(1)}, u32[]{:S(2)}, u32[]{:S(2)}) collective-permute-start(bf16[1,16,2,8,256]{4,1,3,2,0:T(8,128)(2,1)S(1)} %reverse_select_fusion), channel_id=1, source_target_pairs={{0,1},{1,0},{2,3},{3,2},{4,5},{5,4},{6,7},{7,6},{8,9},{9,8},{10,11... | collective-permute-start | bytes 393224 | tf_op jit(solution)/shard_map/ppermute | solution.py:23
  17.8 7.8 %collective-permute-start.1 = (bf16[1,16,2,8,256]{4,1,3,2,0:T(8,128)(2,1)S(1)}, bf16[1,16,2,8,256]{4,1,3,2,0:T(8,128)(2,1)S(1)}, u32[]{:S(2)}, u32[]{:S(2)}) collective-permute-start(bf16[1,16,2,8,256]{4,1,3,2,0:T(8,128)(2,1)S(1)} %broadcast_select_fusion.5), channel_id=1, source_target_pairs={{0,2},{2,0},{1,3},{3,1},{4,6},{6,4},{5,7},{7,5},{8,10},{10,8},{9,1... | collective-permute-start | bytes 393224 | tf_op jit(solution)/shard_map/ppermute | solution.py:23
  25.6 6.9 %collective-permute-start.2 = (bf16[1,16,2,8,256]{4,1,3,2,0:T(8,128)(2,1)S(1)}, bf16[1,16,2,8,256]{4,1,3,2,0:T(8,128)(2,1)S(1)}, u32[]{:S(2)}, u32[]{:S(2)}) collective-permute-start(bf16[1,16,2,8,256]{4,1,3,2,0:T(8,128)(2,1)S(1)} %broadcast_select_fusion.4), channel_id=1, source_target_pairs={{0,4},{4,0},{1,5},{5,1},{2,6},{6,2},{3,7},{7,3},{8,12},{12,8},{9,1... | collective-permute-start | bytes 393224 | tf_op jit(solution)/shard_map/ppermute | solution.py:23
  32.5 9.3 %collective-permute-start.3 = (bf16[1,16,2,8,256]{4,1,3,2,0:T(8,128)(2,1)S(1)}, bf16[1,16,2,8,256]{4,1,3,2,0:T(8,128)(2,1)S(1)}, u32[]{:S(2)}, u32[]{:S(2)}) collective-permute-start(bf16[1,16,2,8,256]{4,1,3,2,0:T(8,128)(2,1)S(1)} %broadcast_select_fusion.3), channel_id=1, source_target_pairs={{0,8},{8,0},{1,9},{9,1},{2,10},{10,2},{3,11},{11,3},{4,12},{12,4},... | collective-permute-start | bytes 393224 | tf_op jit(solution)/shard_map/ppermute | solution.py:23
  41.9 10.9 %collective-permute-start.4 = (bf16[1,16,2,8,256]{4,1,3,2,0:T(8,128)(2,1)S(1)}, bf16[1,16,2,8,256]{4,1,3,2,0:T(8,128)(2,1)S(1)}, u32[]{:S(2)}, u32[]{:S(2)}) collective-permute-start(bf16[1,16,2,8,256]{4,1,3,2,0:T(8,128)(2,1)S(1)} %broadcast_select_fusion.2), channel_id=1, source_target_pairs={{0,16},{16,0},{1,17},{17,1},{2,18},{18,2},{3,19},{19,3},{4,20},{20... | collective-permute-start | bytes 393224 | tf_op jit(solution)/shard_map/ppermute | solution.py:23
  52.7 9.9 %collective-permute-start.5 = (bf16[1,16,2,8,256]{4,1,3,2,0:T(8,128)(2,1)S(1)}, bf16[1,16,2,8,256]{4,1,3,2,0:T(8,128)(2,1)S(1)}, u32[]{:S(2)}, u32[]{:S(2)}) collective-permute-start(bf16[1,16,2,8,256]{4,1,3,2,0:T(8,128)(2,1)S(1)} %broadcast_select_fusion.1), channel_id=1, source_target_pairs={{0,32},{32,0},{1,33},{33,1},{2,34},{34,2},{3,35},{35,3},{4,36},{36... | collective-permute-start | bytes 393224 | tf_op jit(solution)/shard_map/ppermute | solution.py:23
  62.6 20.8 %collective-permute-start.6 = (bf16[1,16,2,8,256]{4,1,3,2,0:T(8,128)(2,1)S(1)}, bf16[1,16,2,8,256]{4,1,3,2,0:T(8,128)(2,1)S(1)}, u32[]{:S(2)}, u32[]{:S(2)}) collective-permute-start(bf16[1,16,2,8,256]{4,1,3,2,0:T(8,128)(2,1)S(1)} %broadcast_select_fusion), channel_id=1, source_target_pairs={{0,1},{1,2},{2,3},{3,4},{4,5},{5,6},{6,7},{7,8},{8,9},{9,10},{10,1... | collective-permute-start | bytes 393224 | tf_op jit(solution)/shard_map/ppermute | solution.py:29
  83.4 61.2 %copy-start.1 = (bf16[27,16,16]{0,2,1:T(8,128)(2,1)S(1)}, bf16[27,16,16]{0,2,1:T(8,128)(2,1)}, u32[]{:S(2)}) copy-start(bf16[27,16,16]{0,2,1:T(8,128)(2,1)} %param.9) | copy-start | bytes 41476
  83.4 14.1 %collective-permute-start.7 = (bf16[1,16,2,8,256]{4,1,3,2,0:T(8,128)(2,1)S(1)}, bf16[1,16,2,8,256]{4,1,3,2,0:T(8,128)(2,1)S(1)}, u32[]{:S(2)}, u32[]{:S(2)}) collective-permute-start(bf16[1,16,2,8,256]{4,1,3,2,0:T(8,128)(2,1)S(1)} %broadcast_select_fusion.6), channel_id=1, source_target_pairs={{0,2},{1,3},{2,4},{3,5},{4,6},{5,7},{6,8},{7,9},{8,10},{9,11},{10,... | collective-permute-start | bytes 393224 | tf_op jit(solution)/shard_map/ppermute | solution.py:29
  97.6 11.7 %collective-permute-start.8 = (bf16[1,16,2,8,256]{4,1,3,2,0:T(8,128)(2,1)S(1)}, bf16[1,16,2,8,256]{4,1,3,2,0:T(8,128)(2,1)S(1)}, u32[]{:S(2)}, u32[]{:S(2)}) collective-permute-start(bf16[1,16,2,8,256]{4,1,3,2,0:T(8,128)(2,1)S(1)} %broadcast_select_fusion.7), channel_id=1, source_target_pairs={{0,4},{1,5},{2,6},{3,7},{4,8},{5,9},{6,10},{7,11},{8,12},{9,13},{1... | collective-permute-start | bytes 393224 | tf_op jit(solution)/shard_map/ppermute | solution.py:29
  109.3 12.6 %collective-permute-start.9 = (bf16[1,16,2,8,256]{4,1,3,2,0:T(8,128)(2,1)S(1)}, bf16[1,16,2,8,256]{4,1,3,2,0:T(8,128)(2,1)S(1)}, u32[]{:S(2)}, u32[]{:S(2)}) collective-permute-start(bf16[1,16,2,8,256]{4,1,3,2,0:T(8,128)(2,1)S(1)} %broadcast_select_fusion.8), channel_id=1, source_target_pairs={{0,8},{1,9},{2,10},{3,11},{4,12},{5,13},{6,14},{7,15},{8,16},{9,17... | collective-permute-start | bytes 393224 | tf_op jit(solution)/shard_map/ppermute | solution.py:29
  122.0 14.4 %collective-permute-start.10 = (bf16[1,16,2,8,256]{4,1,3,2,0:T(8,128)(2,1)S(1)}, bf16[1,16,2,8,256]{4,1,3,2,0:T(8,128)(2,1)S(1)}, u32[]{:S(2)}, u32[]{:S(2)}) collective-permute-start(bf16[1,16,2,8,256]{4,1,3,2,0:T(8,128)(2,1)S(1)} %broadcast_select_fusion.9), channel_id=1, source_target_pairs={{0,16},{1,17},{2,18},{3,19},{4,20},{5,21},{6,22},{7,23},{8,24},{9,... | collective-permute-start | bytes 393224 | tf_op jit(solution)/shard_map/ppermute | solution.py:29
  136.4 10.5 %collective-permute-start.11 = (bf16[1,16,2,8,256]{4,1,3,2,0:T(8,128)(2,1)S(1)}, bf16[1,16,2,8,256]{4,1,3,2,0:T(8,128)(2,1)S(1)}, u32[]{:S(2)}, u32[]{:S(2)}) collective-permute-start(bf16[1,16,2,8,256]{4,1,3,2,0:T(8,128)(2,1)S(1)} %broadcast_select_fusion.10), channel_id=1, source_target_pairs={{0,32},{1,33},{2,34},{3,35},{4,36},{5,37},{6,38},{7,39},{8,40},{9,... | collective-permute-start | bytes 393224 | tf_op jit(solution)/shard_map/ppermute | solution.py:29
  147.0 13.8 %collective-permute-start.12 = (bf16[1,16,2,8,256]{4,1,3,2,0:T(8,128)(2,1)S(1)}, bf16[1,16,2,8,256]{4,1,3,2,0:T(8,128)(2,1)S(1)}, u32[]{:S(2)}, u32[]{:S(2)}) collective-permute-start(bf16[1,16,2,8,256]{4,1,3,2,0:T(8,128)(2,1)S(1)} %broadcast_select_fusion.11), channel_id=1, source_target_pairs={{0,1},{1,2},{2,3},{3,4},{4,5},{5,6},{6,7},{7,8},{8,9},{9,10},{10,1... | collective-permute-start | bytes 393224 | tf_op jit(solution)/shard_map/ppermute | solution.py:29
  160.9 13.6 %collective-permute-start.13 = (bf16[1,16,1,8,256]{4,1,3,2,0:T(8,128)(2,1)S(1)}, bf16[1,16,1,8,256]{4,1,3,2,0:T(8,128)(2,1)S(1)}, u32[]{:S(2)}, u32[]{:S(2)}) collective-permute-start(bf16[1,16,1,8,256]{4,1,3,2,0:T(8,128)(2,1)S(1)} %get-tuple-element.127), channel_id=1, source_target_pairs={{0,1},{1,2},{2,3},{3,4},{4,5},{5,6},{6,7},{7,8},{8,9},{9,10},{10,1... | collective-permute-start | bytes 196616 | tf_op jit(solution)/shard_map/ppermute | solution.py:39
  162.8 12.8 %collective-permute-start.14 = (bf16[1,16,1,8,256]{4,1,3,2,0:T(8,128)(2,1)S(1)}, bf16[1,16,1,8,256]{4,1,3,2,0:T(8,128)(2,1)S(1)}, u32[]{:S(2)}, u32[]{:S(2)}) collective-permute-start(bf16[1,16,1,8,256]{4,1,3,2,0:T(8,128)(2,1)S(1)} %get-tuple-element.128), channel_id=1, source_target_pairs={{1,0},{2,1},{3,2},{4,3},{5,4},{6,5},{7,6},{8,7},{9,8},{10,9},{11,1... | collective-permute-start | bytes 196616 | tf_op jit(solution)/shard_map/ppermute | solution.py:40
  180.8 1.0 copy-start.3
  181.3 1.1 copy-start.2
  311.4 9.0 %collective-permute-start.15 = (bf16[1,16,1,8,256]{4,1,3,2,0:T(8,128)(2,1)S(1)}, bf16[1,16,1,8,256]{4,1,3,2,0:T(8,128)(2,1)S(1)}, u32[]{:S(2)}, u32[]{:S(2)}) collective-permute-start(bf16[1,16,1,8,256]{4,1,3,2,0:T(8,128)(2,1)S(1)} %get-tuple-element.95), channel_id=1, source_target_pairs={{1,0},{2,1},{3,2},{4,3},{5,4},{6,5},{7,6},{8,7},{9,8},{10,9},{11,1... | collective-permute-start | bytes 196616 | tf_op jit(solution)/shard_map/ppermute | solution.py:40
  316.4 13.7 %collective-permute-start.16 = (bf16[1,16,1,8,256]{4,1,3,2,0:T(8,128)(2,1)S(1)}, bf16[1,16,1,8,256]{4,1,3,2,0:T(8,128)(2,1)S(1)}, u32[]{:S(2)}, u32[]{:S(2)}) collective-permute-start(bf16[1,16,1,8,256]{4,1,3,2,0:T(8,128)(2,1)S(1)} %get-tuple-element.96), channel_id=1, source_target_pairs={{0,1},{1,2},{2,3},{3,4},{4,5},{5,6},{6,7},{7,8},{8,9},{9,10},{10,1... | collective-permute-start | bytes 196616 | tf_op jit(solution)/shard_map/ppermute | solution.py:39
where the time goes:
time: 340 us; the launch traced here: 339 us
  blocking collectives  122 us (36%)
  waiting for transfers between devices  96.3 us (28%)
  starting transfers between devices  76.2 us (22%)
  matrix products  18.9 us (6%)
  local copies, waits for them, and re-layouts  14.7 us (4%)
  between operations  5.71 us (2%)
  other arithmetic  5.36 us (2%)
    psum x1, blocking collectives, on_device(): summed_w, summed_b = lax.psum((jnp.stack(grad_list), grad_b), ('dp', 'gx'))  122 us
    ppermute x7, waiting for transfers between devices, shifted(): return lax.ppermute(value, axis, pairs)  69.4 us
    ppermute x6, starting transfers between devices, partner_2(): return lax.ppermute(block, axis, route)  35 us
    ppermute x7, starting transfers between devices, shifted(): return lax.ppermute(value, axis, pairs)  20.9 us
    ppermute x2, starting transfers between devices, padded_2(): after = lax.ppermute(leading, axis, down)  16.5 us
    ppermute x6, waiting for transfers between devices, partner_2(): return lax.ppermute(block, axis, route)  16 us
    ppermute x2, waiting for transfers between devices, padded_2(): before = lax.ppermute(last, axis, up)  9.71 us
    unnamed x38, local copies, waits for them, and re-layouts  7.13 us
  transfers between devices with their start and end apart: 17, of which 15 were waited for; matrix products, arithmetic and copies ran while one was open for 2% of the time, Pallas kernels for 0%

commit v1 on v0

v1 whole, which is shorter than its diff:
```python
import math

import jax
import jax.numpy as jnp
from jax import lax
from jax.sharding import PartitionSpec as P

tap_offsets = [
    (shift_x, shift_y, shift_z)
    for shift_x in range(3)
    for shift_y in range(3)
    for shift_z in range(3)
]


def shifted(value, axis, steps):
    count = lax.axis_size(axis)
    pairs = [(source, (source + steps) % count) for source in range(count)]
    return lax.ppermute(value, axis, pairs)


def mirrored_of(value, axis):
    count = lax.axis_size(axis)
    pairs = [(source, count - 1 - source) for source in range(count)]
    return lax.ppermute(value, axis, pairs)


def butterfly_sum(value, axis):
    count = lax.axis_size(axis)
    step = 1
    while step < count:
        pairs = [(source, source ^ step) for source in range(count)]
        value = value + lax.ppermute(value, axis, pairs)
        step *= 2
    return value


def permute_axis(volume, offset, mirror_bit, length, dim_index):
    position = jnp.arange(length, dtype=jnp.int32)
    source = jnp.where(mirror_bit == 1, length - 1 - position, position)
    source = jnp.mod(source - offset, length)
    return jnp.take(volume, source, axis=dim_index)


def augment_local(volume, offset, mirror_bits):
    volume = permute_axis(volume, offset[1], mirror_bits[1], volume.shape[2], 2)
    return permute_axis(volume, offset[2], mirror_bits[2], volume.shape[3], 3)


def gelu_parts(pre_act):
    normal_cdf = 0.5 * (1.0 + lax.erf(pre_act * 0.7071067811865476))
    density = jnp.exp(-0.5 * pre_act * pre_act) * 0.3989422804014327
    return (pre_act * normal_cdf, normal_cdf + pre_act * density)


def windows(padded, planes, sign):
    out = []
    for shift_x, shift_y, shift_z in tap_offsets:
        start = shift_x if sign > 0 else 2 - shift_x
        piece = padded[:, :, start : start + planes]
        out.append(jnp.roll(piece, (sign * (1 - shift_y), sign * (1 - shift_z)), axis=(3, 4)))
    return jnp.stack(out, 0)


def on_device(features, offsets, flip_bits, weight, conv_bias, cotangent):
    planes = features.shape[2]
    devices_x = lax.axis_size("gx")
    levels = devices_x.bit_length() - 1
    length_x = planes * devices_x
    local = jax.vmap(augment_local)(features, offsets, flip_bits)
    flip_x = flip_bits[0, 0] == 1
    reversed_local = jnp.flip(local, 2)
    mirrored = jnp.where(flip_x, mirrored_of(reversed_local, "gx"), local)
    effective = jnp.where(flip_x, jnp.mod(-offsets[0, 0], length_x), offsets[0, 0])
    coarse_steps = effective // planes
    remain = effective % planes
    coarse = mirrored
    for bit_level in range(levels):
        arrived = shifted(coarse, "gx", 2**bit_level)
        coarse = jnp.where(coarse_steps // 2**bit_level % 2 == 1, arrived, coarse)
    before = shifted(coarse, "gx", 1)
    after = shifted(coarse, "gx", -1)
    joined = jnp.concatenate([before, coarse, after], axis=2)
    padded = lax.dynamic_slice_in_dim(joined, planes - 1 - remain, planes + 2, axis=2)

    taps = len(tap_offsets)
    channels = features.shape[1]
    flat_weight = weight.reshape(taps, channels, channels)
    cols = windows(padded, planes, 1)
    total = jnp.einsum(
        "toi,tbixyz->boxyz", flat_weight, cols, preferred_element_type=jnp.float32
    ) + conv_bias[None, :, None, None, None]
    hidden, slope = gelu_parts(total)
    grad_pre = (cotangent.astype(jnp.float32) * slope).astype(jnp.bfloat16)
    grad_before = shifted(grad_pre[:, :, planes - 1 : planes], "gx", 1)
    grad_after = shifted(grad_pre[:, :, 0:1], "gx", -1)
    grad_w = jnp.einsum("boxyz,tbixyz->toi", grad_pre, cols, preferred_element_type=jnp.float32)
    grad_b = jnp.sum(grad_pre.astype(jnp.float32), axis=(0, 2, 3, 4))
    stacked = jnp.concatenate([grad_w.reshape(-1), grad_b])
    summed = butterfly_sum(butterfly_sum(stacked, "dp"), "gx")
    grad_pad = jnp.concatenate([grad_before, grad_pre, grad_after], axis=2)
    moved = windows(grad_pad, planes, -1)
    grad_in = jnp.einsum(
        "toi,tboxyz->bixyz", flat_weight, moved, preferred_element_type=jnp.float32
    )
    cell_count = (
        features.shape[0] * lax.axis_size("dp") * length_x * features.shape[3] * features.shape[4]
    )
    grad_scale = 1.0 / math.sqrt(cell_count)
    summed = summed * grad_scale
    weight_count = taps * channels * channels
    return (
        hidden.astype(jnp.bfloat16),
        grad_in.astype(jnp.bfloat16),
        summed[:weight_count].reshape(taps, channels, channels),
        summed[weight_count:],
    )


def solution(mesh):
    in_specs = (
        P("dp", None, "gx", None, None),
        P("dp", None),
        P("dp", None),
        P(),
        P(),
        P("dp", None, "gx", None, None),
    )
    out_specs = (P("dp", None, "gx", None, None), P("dp", None, "gx", None, None), P(), P())
    return jax.shard_map(
        on_device, mesh=mesh, in_specs=in_specs, out_specs=out_specs, check_vma=False
    )
```

time: 340 us -> 272 us (0.80)
  the two profiles are of different devices: /device:TPU:1 before, /device:TPU:16 now
where the time goes in v1:
time: 272 us; the launch traced here: 270 us
  waiting for transfers between devices  113 us (42%)
  starting transfers between devices  85.1 us (31%)
  local copies, waits for them, and re-layouts  49.5 us (18%)
  other arithmetic  9.62 us (4%)
  matrix products  7.02 us (3%)
  between operations  5.76 us (2%)
    ppermute x10, waiting for transfers between devices, shifted(): return lax.ppermute(value, axis, pairs)  75.2 us
    ppermute x10, starting transfers between devices, shifted(): return lax.ppermute(value, axis, pairs)  42.5 us
    another operation x29, local copies, waits for them, and re-layouts, windows(): return jnp.stack(out, 0)  38.7 us
    ppermute x9, waiting for transfers between devices, butterfly_sum(): value = value + lax.ppermute(value, axis, pairs)  31.9 us
    ppermute x9, starting transfers between devices, butterfly_sum(): value = value + lax.ppermute(value, axis, pairs)  26 us
    ppermute x1, starting transfers between devices, mirrored_of(): return lax.ppermute(value, axis, pairs)  16.6 us
    ppermute x1, waiting for transfers between devices, mirrored_of(): return lax.ppermute(value, axis, pairs)  5.64 us
  transfers between devices with their start and end apart: 20, of which 16 were waited for; matrix products, arithmetic and copies ran while one was open for 2% of the time, Pallas kernels for 0%

profile of v1, /device:TPU:16, one launch (start us, length us, event | category | flops | bytes accessed | tf_op | source)
XLA Modules:
  0.0 269.8 jit_solution(6287768760523224719)
XLA Ops:
  10.8 16.6 %collective-permute-start = (bf16[1,16,2,8,256]{4,3,2,1,0:T(8,128)(2,1)S(1)}, bf16[1,16,2,8,256]{4,3,2,1,0:T(8,128)(2,1)S(1)}, u32[]{:S(2)}, u32[]{:S(2)}) collective-permute-start(bf16[1,16,2,8,256]{4,3,2,1,0:T(8,128)(2,1)S(1)} %rev.4), channel_id=1, source_target_pairs={{0,63},{1,62},{2,61},{3,60},{4,59},{5,58},{6,57},{7,56},{8,55},{9,... | collective-permute-start | bytes 393224 | tf_op jit(solution)/shard_map/ppermute | solution.py:25
  28.1 5.6 %collective-permute-done = bf16[1,16,2,8,256]{4,3,2,1,0:T(8,128)(2,1)S(1)} collective-permute-done((bf16[1,16,2,8,256]{4,3,2,1,0:T(8,128)(2,1)S(1)}, bf16[1,16,2,8,256]{4,3,2,1,0:T(8,128)(2,1)S(1)}, u32[]{:S(2)}, u32[]{:S(2)}) %collective-permute-start) | collective-permute-done | bytes 131104 | tf_op jit(solution)/shard_map/ppermute | solution.py:25
  33.7 2.1 collective-permute-start.1
  37.9 11.3 %collective-permute-done.1 = bf16[1,16,2,8,256]{4,3,2,1,0:T(8,128)(2,1)S(1)} collective-permute-done((bf16[1,16,2,8,256]{4,3,2,1,0:T(8,128)(2,1)S(1)}, bf16[1,16,2,8,256]{4,3,2,1,0:T(8,128)(2,1)S(1)}, u32[]{:S(2)}, u32[]{:S(2)}) %collective-permute-start.1) | collective-permute-done | bytes 131104 | tf_op jit(solution)/shard_map/ppermute | solution.py:19
  49.3 1.9 collective-permute-start.2
  51.3 14.9 %collective-permute-done.2 = bf16[1,16,2,8,256]{4,3,2,1,0:T(8,128)(2,1)S(1)} collective-permute-done((bf16[1,16,2,8,256]{4,3,2,1,0:T(8,128)(2,1)S(1)}, bf16[1,16,2,8,256]{4,3,2,1,0:T(8,128)(2,1)S(1)}, u32[]{:S(2)}, u32[]{:S(2)}) %collective-permute-start.2) | collective-permute-done | bytes 131104 | tf_op jit(solution)/shard_map/ppermute | solution.py:19
  66.2 1.9 collective-permute-start.3
  68.2 12.1 %collective-permute-done.3 = bf16[1,16,2,8,256]{4,3,2,1,0:T(8,128)(2,1)S(1)} collective-permute-done((bf16[1,16,2,8,256]{4,3,2,1,0:T(8,128)(2,1)S(1)}, bf16[1,16,2,8,256]{4,3,2,1,0:T(8,128)(2,1)S(1)}, u32[]{:S(2)}, u32[]{:S(2)}) %collective-permute-start.3) | collective-permute-done | bytes 131104 | tf_op jit(solution)/shard_map/ppermute | solution.py:19
  80.3 1.9 collective-permute-start.4
  82.3 14.2 %collective-permute-done.4 = bf16[1,16,2,8,256]{4,3,2,1,0:T(8,128)(2,1)S(1)} collective-permute-done((bf16[1,16,2,8,256]{4,3,2,1,0:T(8,128)(2,1)S(1)}, bf16[1,16,2,8,256]{4,3,2,1,0:T(8,128)(2,1)S(1)}, u32[]{:S(2)}, u32[]{:S(2)}) %collective-permute-start.4) | collective-permute-done | bytes 131104 | tf_op jit(solution)/shard_map/ppermute | solution.py:19
  96.6 1.9 collective-permute-start.5
  98.5 13.6 %collective-permute-done.5 = bf16[1,16,2,8,256]{4,3,2,1,0:T(8,128)(2,1)S(1)} collective-permute-done((bf16[1,16,2,8,256]{4,3,2,1,0:T(8,128)(2,1)S(1)}, bf16[1,16,2,8,256]{4,3,2,1,0:T(8,128)(2,1)S(1)}, u32[]{:S(2)}, u32[]{:S(2)}) %collective-permute-start.5) | collective-permute-done | bytes 131104 | tf_op jit(solution)/shard_map/ppermute | solution.py:19
  112.2 4.2 %collective-permute-start.6 = (bf16[1,16,2,8,256]{4,3,2,1,0:T(8,128)(2,1)S(1)}, bf16[1,16,2,8,256]{4,3,2,1,0:T(8,128)(2,1)S(1)}, u32[]{:S(2)}, u32[]{:S(2)}) collective-permute-start(bf16[1,16,2,8,256]{4,3,2,1,0:T(8,128)(2,1)S(1)} %broadcast_select_fusion.5), channel_id=1, source_target_pairs={{0,32},{1,33},{2,34},{3,35},{4,36},{5,37},{6,38},{7,39},{8,40},{9,... | collective-permute-start | bytes 393224 | tf_op jit(solution)/shard_map/ppermute | solution.py:19
  116.4 6.6 %collective-permute-done.6 = bf16[1,16,2,8,256]{4,3,2,1,0:T(8,128)(2,1)S(1)} collective-permute-done((bf16[1,16,2,8,256]{4,3,2,1,0:T(8,128)(2,1)S(1)}, bf16[1,16,2,8,256]{4,3,2,1,0:T(8,128)(2,1)S(1)}, u32[]{:S(2)}, u32[]{:S(2)}) %collective-permute-start.6) | collective-permute-done | bytes 131104 | tf_op jit(solution)/shard_map/ppermute | solution.py:19
  123.0 1.9 collective-permute-start.7
  125.0 12.2 %collective-permute-start.8 = (bf16[1,16,2,8,256]{4,3,2,1,0:T(8,128)(2,1)S(1)}, bf16[1,16,2,8,256]{4,3,2,1,0:T(8,128)(2,1)S(1)}, u32[]{:S(2)}, u32[]{:S(2)}) collective-permute-start(bf16[1,16,2,8,256]{4,3,2,1,0:T(8,128)(2,1)S(1)} %broadcast_select_fusion.6), channel_id=1, source_target_pairs={{0,63},{1,0},{2,1},{3,2},{4,3},{5,4},{6,5},{7,6},{8,7},{9,8},{10,9... | collective-permute-start | bytes 393224 | tf_op jit(solution)/shard_map/ppermute | solution.py:19
  160.3 22.4 %stack.195 = bf16[27,1,16,2,8,256]{5,0,2,4,3,1:T(8,128)(2,1)} concatenate(bf16[1,1,16,2,8,256]{5,0,2,4,3,1:T(2,128)(2,1)} %copy.1345, bf16[1,1,16,2,8,256]{5,0,2,4,3,1:T(2,128)(2,1)} %copy.1346, bf16[1,1,16,2,8,256]{5,0,2,4,3,1:T(2,128)(2,1)} %copy.1347, bf16[1,1,16,2,8,256]{5,0,2,4,3,1:T(2,128)(2,1)} %copy.1348, bf16[1,1,16,2,8,256]{5,0,2,4,3,1:T(2,128)(2,1)} %copy.1349, ...), dimensions={0} | concatenate | bytes 7077888 | tf_op jit(solution)/shard_map/stack | solution.py:62
  182.7 3.2 %convert_reduce_fusion = (f32[16]{0:T(128)S(1)}, bf16[1,16,2,8,256]{4,1,3,2,0:T(8,128)(2,1)S(1)}, bf16[1,16,2,8,256]{4,1,3,2,0:T(8,128)(2,1)S(1)}) fusion(bf16[1,16,2,8,256]{4,3,2,1,0:T(8,128)(2,1)} %param.11, f32[16]{0:T(128)S(1)} %copy-done.3, bf16[27,16,16,1,1]{0,2,1,4,3:T(8,128)(2,1)} %bitcast.237, bf16[27,1,16,2,8,256]{5,0,2,4,3,1:T(8,128)(2,1)} %stack.195), kind=kOutput, calls=%fused_computation.107 | convolution fusion | flops 57671664 | bytes 3946112 | tf_op jit(solution)/shard_map/toi,tbixyz->boxyz/dot_general | solution.py:90
  186.3 2.8 %fusion.15 = f32[27,16,16]{0,1,2:T(8,128)S(1)} fusion(bf16[27,1,16,2,8,256]{5,0,2,4,3,1:T(8,128)(2,1)S(1)} %copy-done.1, bf16[1,16,2,8,256]{4,1,3,2,0:T(8,128)(2,1)S(1)} %get-tuple-element.117), kind=kOutput, calls=%fused_computation.11 | convolution fusion | flops 56623104 | bytes 3697664 | tf_op jit(solution)/shard_map/boxyz,tbixyz->toi/dot_general | solution.py:97
  189.4 1.9 collective-permute-start.11
  191.4 1.9 collective-permute-start.10
  193.3 12.5 %collective-permute-start.9 = (bf16[1,16,1,8,256]{4,1,3,2,0:T(8,128)(2,1)S(1)}, bf16[1,16,1,8,256]{4,1,3,2,0:T(8,128)(2,1)S(1)}, u32[]{:S(2)}, u32[]{:S(2)}) collective-permute-start(bf16[1,16,1,8,256]{4,1,3,2,0:T(8,128)(2,1)S(1)} %get-tuple-element.209), channel_id=1, source_target_pairs={{0,63},{1,0},{2,1},{3,2},{4,3},{5,4},{6,5},{7,6},{8,7},{9,8},{10,9... | collective-permute-start | bytes 196616 | tf_op jit(solution)/shard_map/ppermute | solution.py:19
  205.8 6.0 %collective-permute-start.12 = (f32[6928]{0:T(1024)S(1)}, f32[6928]{0:T(1024)S(1)}, u32[]{:S(2)}, u32[]{:S(2)}) collective-permute-start(f32[6928]{0:T(1024)S(1)} %fusion.146), channel_id=1, source_target_pairs={{0,128},{64,192},{128,0},{192,64},{256,384},{320,448},{384,256},{4... | collective-permute-start | bytes 83144 | tf_op jit(solution)/shard_map/ppermute | solution.py:33
  214.2 5.9 %collective-permute-start.13 = (f32[6928]{0:T(1024)S(1)}, f32[6928]{0:T(1024)S(1)}, u32[]{:S(2)}, u32[]{:S(2)}) collective-permute-start(f32[6928]{0:T(1024)S(1)} %add.205), channel_id=1, source_target_pairs={{0,256},{64,320},{128,384},{192,448},{256,0},{320,64},{384,128},{4... | collective-permute-start | bytes 83144 | tf_op jit(solution)/shard_map/ppermute | solution.py:33
  223.5 1.9 collective-permute-start.14
  225.4 3.8 %collective-permute-done.14 = f32[6928]{0:T(1024)S(1)} collective-permute-done((f32[6928]{0:T(1024)S(1)}, f32[6928]{0:T(1024)S(1)}, u32[]{:S(2)}, u32[]{:S(2)}) %collective-permute-start.14) | collective-permute-done | bytes 27744 | tf_op jit(solution)/shard_map/ppermute | solution.py:33
  231.3 5.2 %collective-permute-done.15 = f32[6928]{0:T(1024)S(1)} collective-permute-done((f32[6928]{0:T(1024)S(1)}, f32[6928]{0:T(1024)S(1)}, u32[]{:S(2)}, u32[]{:S(2)}) %collective-permute-start.15) | collective-permute-done | bytes 27744 | tf_op jit(solution)/shard_map/ppermute | solution.py:33
  238.6 3.7 %collective-permute-done.16 = f32[6928]{0:T(1024)S(1)} collective-permute-done((f32[6928]{0:T(1024)S(1)}, f32[6928]{0:T(1024)S(1)}, u32[]{:S(2)}, u32[]{:S(2)}) %collective-permute-start.16) | collective-permute-done | bytes 27744 | tf_op jit(solution)/shard_map/ppermute | solution.py:33
  244.2 4.7 %collective-permute-done.17 = f32[6928]{0:T(1024)S(1)} collective-permute-done((f32[6928]{0:T(1024)S(1)}, f32[6928]{0:T(1024)S(1)}, u32[]{:S(2)}, u32[]{:S(2)}) %collective-permute-start.17) | collective-permute-done | bytes 27744 | tf_op jit(solution)/shard_map/ppermute | solution.py:33
  251.0 7.6 %collective-permute-done.18 = f32[6928]{0:T(1024)S(1)} collective-permute-done((f32[6928]{0:T(1024)S(1)}, f32[6928]{0:T(1024)S(1)}, u32[]{:S(2)}, u32[]{:S(2)}) %collective-permute-start.18) | collective-permute-done | bytes 27744 | tf_op jit(solution)/shard_map/ppermute | solution.py:33
  258.6 2.6 collective-permute-start.19
  263.0 5.3 %collective-permute-done.19 = f32[6928]{0:T(1024)S(1)} collective-permute-done((f32[6928]{0:T(1024)S(1)}, f32[6928]{0:T(1024)S(1)}, u32[]{:S(2)}, u32[]{:S(2)}) %collective-permute-start.19) | collective-permute-done | bytes 27744 | tf_op jit(solution)/shard_map/ppermute | solution.py:33
  (165 shorter events, 49.1 us)
Async XLA Ops:
  0.6 6.5 %copy-start = (bf16[1,16,2,8,256]{4,3,2,1,0:T(8,128)(2,1)S(1)}, bf16[1,16,2,8,256]{4,3,2,1,0:T(8,128)(2,1)}, u32[]{:S(2)}) copy-start(bf16[1,16,2,8,256]{4,3,2,1,0:T(8,128)(2,1)} %param.6) | copy-start | bytes 393220
  10.8 22.9 %collective-permute-start = (bf16[1,16,2,8,256]{4,3,2,1,0:T(8,128)(2,1)S(1)}, bf16[1,16,2,8,256]{4,3,2,1,0:T(8,128)(2,1)S(1)}, u32[]{:S(2)}, u32[]{:S(2)}) collective-permute-start(bf16[1,16,2,8,256]{4,3,2,1,0:T(8,128)(2,1)S(1)} %rev.4), channel_id=1, source_target_pairs={{0,63},{1,62},{2,61},{3,60},{4,59},{5,58},{6,57},{7,56},{8,55},{9,... | collective-permute-start | bytes 393224 | tf_op jit(solution)/shard_map/ppermute | solution.py:25
  33.7 15.5 %collective-permute-start.1 = (bf16[1,16,2,8,256]{4,3,2,1,0:T(8,128)(2,1)S(1)}, bf16[1,16,2,8,256]{4,3,2,1,0:T(8,128)(2,1)S(1)}, u32[]{:S(2)}, u32[]{:S(2)}) collective-permute-start(bf16[1,16,2,8,256]{4,3,2,1,0:T(8,128)(2,1)S(1)} %broadcast_select_fusion), channel_id=1, source_target_pairs={{0,1},{1,2},{2,3},{3,4},{4,5},{5,6},{6,7},{7,8},{8,9},{9,10},{10,1... | collective-permute-start | bytes 393224 | tf_op jit(solution)/shard_map/ppermute | solution.py:19
  49.3 16.9 %collective-permute-start.2 = (bf16[1,16,2,8,256]{4,3,2,1,0:T(8,128)(2,1)S(1)}, bf16[1,16,2,8,256]{4,3,2,1,0:T(8,128)(2,1)S(1)}, u32[]{:S(2)}, u32[]{:S(2)}) collective-permute-start(bf16[1,16,2,8,256]{4,3,2,1,0:T(8,128)(2,1)S(1)} %broadcast_select_fusion.1), channel_id=1, source_target_pairs={{0,2},{1,3},{2,4},{3,5},{4,6},{5,7},{6,8},{7,9},{8,10},{9,11},{10,... | collective-permute-start | bytes 393224 | tf_op jit(solution)/shard_map/ppermute | solution.py:19
  66.2 14.1 %collective-permute-start.3 = (bf16[1,16,2,8,256]{4,3,2,1,0:T(8,128)(2,1)S(1)}, bf16[1,16,2,8,256]{4,3,2,1,0:T(8,128)(2,1)S(1)}, u32[]{:S(2)}, u32[]{:S(2)}) collective-permute-start(bf16[1,16,2,8,256]{4,3,2,1,0:T(8,128)(2,1)S(1)} %broadcast_select_fusion.2), channel_id=1, source_target_pairs={{0,4},{1,5},{2,6},{3,7},{4,8},{5,9},{6,10},{7,11},{8,12},{9,13},{1... | collective-permute-start | bytes 393224 | tf_op jit(solution)/shard_map/ppermute | solution.py:19
  80.3 16.2 %collective-permute-start.4 = (bf16[1,16,2,8,256]{4,3,2,1,0:T(8,128)(2,1)S(1)}, bf16[1,16,2,8,256]{4,3,2,1,0:T(8,128)(2,1)S(1)}, u32[]{:S(2)}, u32[]{:S(2)}) collective-permute-start(bf16[1,16,2,8,256]{4,3,2,1,0:T(8,128)(2,1)S(1)} %broadcast_select_fusion.3), channel_id=1, source_target_pairs={{0,8},{1,9},{2,10},{3,11},{4,12},{5,13},{6,14},{7,15},{8,16},{9,17... | collective-permute-start | bytes 393224 | tf_op jit(solution)/shard_map/ppermute | solution.py:19
  96.6 15.6 %collective-permute-start.5 = (bf16[1,16,2,8,256]{4,3,2,1,0:T(8,128)(2,1)S(1)}, bf16[1,16,2,8,256]{4,3,2,1,0:T(8,128)(2,1)S(1)}, u32[]{:S(2)}, u32[]{:S(2)}) collective-permute-start(bf16[1,16,2,8,256]{4,3,2,1,0:T(8,128)(2,1)S(1)} %broadcast_select_fusion.4), channel_id=1, source_target_pairs={{0,16},{1,17},{2,18},{3,19},{4,20},{5,21},{6,22},{7,23},{8,24},{9,... | collective-permute-start | bytes 393224 | tf_op jit(solution)/shard_map/ppermute | solution.py:19
  112.2 10.8 %collective-permute-start.6 = (bf16[1,16,2,8,256]{4,3,2,1,0:T(8,128)(2,1)S(1)}, bf16[1,16,2,8,256]{4,3,2,1,0:T(8,128)(2,1)S(1)}, u32[]{:S(2)}, u32[]{:S(2)}) collective-permute-start(bf16[1,16,2,8,256]{4,3,2,1,0:T(8,128)(2,1)S(1)} %broadcast_select_fusion.5), channel_id=1, source_target_pairs={{0,32},{1,33},{2,34},{3,35},{4,36},{5,37},{6,38},{7,39},{8,40},{9,... | collective-permute-start | bytes 393224 | tf_op jit(solution)/shard_map/ppermute | solution.py:19
  123.0 15.0 %collective-permute-start.7 = (bf16[1,16,2,8,256]{4,3,2,1,0:T(8,128)(2,1)S(1)}, bf16[1,16,2,8,256]{4,3,2,1,0:T(8,128)(2,1)S(1)}, u32[]{:S(2)}, u32[]{:S(2)}) collective-permute-start(bf16[1,16,2,8,256]{4,3,2,1,0:T(8,128)(2,1)S(1)} %broadcast_select_fusion.6), channel_id=1, source_target_pairs={{0,1},{1,2},{2,3},{3,4},{4,5},{5,6},{6,7},{7,8},{8,9},{9,10},{10,1... | collective-permute-start | bytes 393224 | tf_op jit(solution)/shard_map/ppermute | solution.py:19
  125.0 14.6 %collective-permute-start.8 = (bf16[1,16,2,8,256]{4,3,2,1,0:T(8,128)(2,1)S(1)}, bf16[1,16,2,8,256]{4,3,2,1,0:T(8,128)(2,1)S(1)}, u32[]{:S(2)}, u32[]{:S(2)}) collective-permute-start(bf16[1,16,2,8,256]{4,3,2,1,0:T(8,128)(2,1)S(1)} %broadcast_select_fusion.6), channel_id=1, source_target_pairs={{0,63},{1,0},{2,1},{3,2},{4,3},{5,4},{6,5},{7,6},{8,7},{9,8},{10,9... | collective-permute-start | bytes 393224 | tf_op jit(solution)/shard_map/ppermute | solution.py:19
  160.3 22.5 %copy-start.3 = (f32[16]{0:T(128)S(1)}, f32[16]{0:T(128)}, u32[]{:S(2)}) copy-start(f32[16]{0:T(128)} %param.10) | copy-start | bytes 196
  182.7 3.5 %copy-start.1 = (bf16[27,1,16,2,8,256]{5,0,2,4,3,1:T(8,128)(2,1)S(1)}, bf16[27,1,16,2,8,256]{5,0,2,4,3,1:T(8,128)(2,1)}, u32[]{:S(2)}) copy-start(bf16[27,1,16,2,8,256]{5,0,2,4,3,1:T(8,128)(2,1)} %stack.195) | copy-start | bytes 10616836
  186.0 25.8 %copy-start.2 = (bf16[27,16,16]{0,2,1:T(8,128)(2,1)S(1)}, bf16[27,16,16]{0,2,1:T(8,128)(2,1)}, u32[]{:S(2)}) copy-start(bf16[27,16,16]{0,2,1:T(8,128)(2,1)} %param.9) | copy-start | bytes 41476
  189.4 16.4 %collective-permute-start.11 = (f32[6928]{0:T(1024)S(1)}, f32[6928]{0:T(1024)S(1)}, u32[]{:S(2)}, u32[]{:S(2)}) collective-permute-start(f32[6928]{0:T(1024)S(1)} %pad_maximum_fusion.12), channel_id=1, source_target_pairs={{0,64},{64,0},{128,192},{192,128},{256,320},{320,256},{384,448},{4... | collective-permute-start | bytes 83144 | tf_op jit(solution)/shard_map/ppermute | solution.py:33
  191.4 28.7 %collective-permute-start.10 = (bf16[1,16,1,8,256]{4,1,3,2,0:T(8,128)(2,1)S(1)}, bf16[1,16,1,8,256]{4,1,3,2,0:T(8,128)(2,1)S(1)}, u32[]{:S(2)}, u32[]{:S(2)}) collective-permute-start(bf16[1,16,1,8,256]{4,1,3,2,0:T(8,128)(2,1)S(1)} %get-tuple-element.208), channel_id=1, source_target_pairs={{0,1},{1,2},{2,3},{3,4},{4,5},{5,6},{6,7},{7,8},{8,9},{9,10},{10,1... | collective-permute-start | bytes 196616 | tf_op jit(solution)/shard_map/ppermute | solution.py:19
  193.3 26.8 %collective-permute-start.9 = (bf16[1,16,1,8,256]{4,1,3,2,0:T(8,128)(2,1)S(1)}, bf16[1,16,1,8,256]{4,1,3,2,0:T(8,128)(2,1)S(1)}, u32[]{:S(2)}, u32[]{:S(2)}) collective-permute-start(bf16[1,16,1,8,256]{4,1,3,2,0:T(8,128)(2,1)S(1)} %get-tuple-element.209), channel_id=1, source_target_pairs={{0,63},{1,0},{2,1},{3,2},{4,3},{5,4},{6,5},{7,6},{8,7},{9,8},{10,9... | collective-permute-start | bytes 196616 | tf_op jit(solution)/shard_map/ppermute | solution.py:19
  205.8 8.3 %collective-permute-start.12 = (f32[6928]{0:T(1024)S(1)}, f32[6928]{0:T(1024)S(1)}, u32[]{:S(2)}, u32[]{:S(2)}) collective-permute-start(f32[6928]{0:T(1024)S(1)} %fusion.146), channel_id=1, source_target_pairs={{0,128},{64,192},{128,0},{192,64},{256,384},{320,448},{384,256},{4... | collective-permute-start | bytes 83144 | tf_op jit(solution)/shard_map/ppermute | solution.py:33
  214.2 9.3 %collective-permute-start.13 = (f32[6928]{0:T(1024)S(1)}, f32[6928]{0:T(1024)S(1)}, u32[]{:S(2)}, u32[]{:S(2)}) collective-permute-start(f32[6928]{0:T(1024)S(1)} %add.205), channel_id=1, source_target_pairs={{0,256},{64,320},{128,384},{192,448},{256,0},{320,64},{384,128},{4... | collective-permute-start | bytes 83144 | tf_op jit(solution)/shard_map/ppermute | solution.py:33
  223.5 5.8 %collective-permute-start.14 = (f32[6928]{0:T(1024)S(1)}, f32[6928]{0:T(1024)S(1)}, u32[]{:S(2)}, u32[]{:S(2)}) collective-permute-start(f32[6928]{0:T(1024)S(1)} %add.206), channel_id=1, source_target_pairs={{0,1},{1,0},{2,3},{3,2},{4,5},{5,4},{6,7},{7,6},{8,9},{9,8},{10,11... | collective-permute-start | bytes 83144 | tf_op jit(solution)/shard_map/ppermute | solution.py:33
  229.3 7.3 %collective-permute-start.15 = (f32[6928]{0:T(1024)S(1)}, f32[6928]{0:T(1024)S(1)}, u32[]{:S(2)}, u32[]{:S(2)}) collective-permute-start(f32[6928]{0:T(1024)S(1)} %add.207), channel_id=1, source_target_pairs={{0,2},{1,3},{2,0},{3,1},{4,6},{5,7},{6,4},{7,5},{8,10},{9,11},{10,... | collective-permute-start | bytes 83144 | tf_op jit(solution)/shard_map/ppermute | solution.py:33
  236.5 5.8 %collective-permute-start.16 = (f32[6928]{0:T(1024)S(1)}, f32[6928]{0:T(1024)S(1)}, u32[]{:S(2)}, u32[]{:S(2)}) collective-permute-start(f32[6928]{0:T(1024)S(1)} %add.208), channel_id=1, source_target_pairs={{0,4},{1,5},{2,6},{3,7},{4,0},{5,1},{6,2},{7,3},{8,12},{9,13},{10,... | collective-permute-start | bytes 83144 | tf_op jit(solution)/shard_map/ppermute | solution.py:33
  242.3 6.7 %collective-permute-start.17 = (f32[6928]{0:T(1024)S(1)}, f32[6928]{0:T(1024)S(1)}, u32[]{:S(2)}, u32[]{:S(2)}) collective-permute-start(f32[6928]{0:T(1024)S(1)} %add.209), channel_id=1, source_target_pairs={{0,8},{1,9},{2,10},{3,11},{4,12},{5,13},{6,14},{7,15},{8,0},{9,1},... | collective-permute-start | bytes 83144 | tf_op jit(solution)/shard_map/ppermute | solution.py:33
  249.0 9.7 %collective-permute-start.18 = (f32[6928]{0:T(1024)S(1)}, f32[6928]{0:T(1024)S(1)}, u32[]{:S(2)}, u32[]{:S(2)}) collective-permute-start(f32[6928]{0:T(1024)S(1)} %add.210), channel_id=1, source_target_pairs={{0,16},{1,17},{2,18},{3,19},{4,20},{5,21},{6,22},{7,23},{8,24},{9,... | collective-permute-start | bytes 83144 | tf_op jit(solution)/shard_map/ppermute | solution.py:33
  258.6 9.7 %collective-permute-start.19 = (f32[6928]{0:T(1024)S(1)}, f32[6928]{0:T(1024)S(1)}, u32[]{:S(2)}, u32[]{:S(2)}) collective-permute-start(f32[6928]{0:T(1024)S(1)} %add.211), channel_id=1, source_target_pairs={{0,32},{1,33},{2,34},{3,35},{4,36},{5,37},{6,38},{7,39},{8,40},{9,... | collective-permute-start | bytes 83144 | tf_op jit(solution)/shard_map/ppermute | solution.py:33
